TPU v7x, 32 devices: a whole 2x2x4 slice. The times are simulated.
32 devices in a mesh: slab: 8 (over z, y), coil: 4 (over x, core).
Axes of the slice: x: 2, y: 2, z: 4, core: 2. Of those that a mesh axis runs over, the one named last changes fastest.
Arguments:
- image: bfloat16 [2, 320, 256, 128], P(None, None, 'slab'), may hold values from -6 to 6
- coil_maps: bfloat16 [16, 320, 256, 128], P('coil', None, 'slab'), may hold values from -5 to 5
- y_data: bfloat16 [2, 16, 320, 128, 128], P(None, 'coil', 'slab'), may hold values from -6 to 6
- kz_lines: int32 [2, 320, 128], P(None, 'slab'), may hold values from -1 to 255, as said below
Outputs:
- gradient: bfloat16 [2, 320, 256, 128], P(None, 'coil', 'slab')
Inputs may be any that keep to these rules, and one draw needn't show every extreme that they name: kz_lines[m, ky, :] lists distinct sampled kz of that ky row first and -1 in the unused slots after them; every row has at least one sampled kz; row 160 uses all 128 slots.
All inputs are finite; a program needn't handle non-finite values.
Results may differ from a plain program's by a relative error of at most 0.0061.
Values may be sent and summed in bfloat16 or wider, within the bound.
No kernel may reach another device: no remote copies, remote signals or barrier semaphores. Data moves between devices by JAX's collectives and lax.ppermute only.
A program may use at most 256 MiB of HBM per device.

v0:
```python
import math
import jax
import jax.numpy as jnp
from jax import lax
from jax.sharding import PartitionSpec as P


def cos_sin(length):
    positions = jnp.arange(length, dtype=jnp.int32)
    phase = (positions[:, None] * positions[None, :] % length).astype(jnp.float32) * (
        2.0 * math.pi / length
    )
    factor = 1.0 / math.sqrt(length)
    return (
        (jnp.cos(phase) * factor).astype(jnp.bfloat16),
        (jnp.sin(phase) * factor).astype(jnp.bfloat16),
    )


def lane_tables(lane_count):
    half_lanes = lane_count // 2
    rows = jnp.arange(lane_count, dtype=jnp.int32)[:, None]
    cols = jnp.arange(lane_count, dtype=jnp.int32)[None, :]
    rotate = jnp.where((rows == cols + half_lanes) & (cols < half_lanes), -1.0, 0.0)
    rotate = rotate + jnp.where((cols == rows + half_lanes) & (rows < half_lanes), 1.0, 0.0)
    same_slot = rows % half_lanes == cols % half_lanes
    dup_real = jnp.where(same_slot & (rows < half_lanes), 1.0, 0.0)
    dup_imag = jnp.where(same_slot & (rows >= half_lanes), 1.0, 0.0)
    return (
        rotate.astype(jnp.bfloat16),
        dup_real.astype(jnp.bfloat16),
        dup_imag.astype(jnp.bfloat16),
    )


def lane_map(values, table):
    if values.dtype == jnp.bfloat16:
        return jnp.einsum("...l,lm->...m", values, table, preferred_element_type=jnp.float32)
    return jnp.einsum(
        "...l,lm->...m", values, table.astype(jnp.float32), precision=lax.Precision.HIGHEST
    )


def transform(image, coil_maps, y_data, kz_lines, forward, backward):
    state_count, y_count, z_local, lane_count = image.shape
    rotate, dup_real, dup_imag = lane_tables(lane_count)
    y_cos, y_sin = cos_sin(y_count)
    sens_real = lane_map(coil_maps, dup_real)[None]
    sens_imag = lane_map(coil_maps, dup_imag)[None]
    pixels = image.astype(jnp.float32)[:, None]
    turned_pixels = lane_map(image, rotate)[:, None]
    coil_image = (sens_real * pixels + sens_imag * turned_pixels).astype(jnp.bfloat16)
    turned_image = lane_map(coil_image, rotate).astype(jnp.bfloat16)
    spectrum = (
        jnp.einsum("ky,scyzl->sckzl", y_cos, coil_image, preferred_element_type=jnp.float32)
        - jnp.einsum("ky,scyzl->sckzl", y_sin, turned_image, preferred_element_type=jnp.float32)
    ).astype(jnp.bfloat16)
    gathered = forward(spectrum)
    z_count = gathered.shape[3]
    z_cos, z_sin = cos_sin(z_count)
    turned_gathered = lane_map(gathered, rotate).astype(jnp.bfloat16)
    sampled = kz_lines >= 0
    kz_index = jnp.maximum(kz_lines, 0)
    onehot = (
        (kz_index[..., None] == jnp.arange(z_count, dtype=jnp.int32)) & sampled[..., None]
    ).astype(jnp.bfloat16)
    measured = y_data.astype(jnp.float32)
    sampled_wide = sampled[:, None, :, :, None]
    kspace = jnp.einsum(
        "jq,sckql->sckjl", z_cos, gathered, preferred_element_type=jnp.float32
    ) - jnp.einsum("jq,sckql->sckjl", z_sin, turned_gathered, preferred_element_type=jnp.float32)
    picked = jnp.einsum(
        "skjq,sckql->sckjl", onehot.astype(jnp.float32), kspace, precision=lax.Precision.HIGHEST
    )
    residual = jnp.where(sampled_wide, picked - measured, jnp.float32(0.0)).astype(jnp.bfloat16)
    kz_grid = jnp.einsum(
        "skjq,sckjl->sckql", onehot, residual, preferred_element_type=jnp.float32
    ).astype(jnp.bfloat16)
    turned_grid = lane_map(kz_grid, rotate).astype(jnp.bfloat16)
    adjoint_z = (
        jnp.einsum("qz,sckql->sckzl", z_cos, kz_grid, preferred_element_type=jnp.float32)
        + jnp.einsum("qz,sckql->sckzl", z_sin, turned_grid, preferred_element_type=jnp.float32)
    ).astype(jnp.bfloat16)
    returned = backward(adjoint_z)
    turned_returned = lane_map(returned, rotate).astype(jnp.bfloat16)
    coil_back = jnp.einsum(
        "ky,sckzl->scyzl", y_cos, returned, preferred_element_type=jnp.float32
    ) + jnp.einsum("ky,sckzl->scyzl", y_sin, turned_returned, preferred_element_type=jnp.float32)
    turned_back = lane_map(coil_back, rotate)
    return jnp.sum(sens_real * coil_back - sens_imag * turned_back, axis=1)


def shards(image, coil_maps, y_data, kz_lines):
    partial_image = transform(
        image,
        coil_maps,
        y_data,
        kz_lines,
        lambda payload: lax.all_to_all(payload, "slab", split_axis=2, concat_axis=3, tiled=True),
        lambda payload: lax.all_to_all(payload, "slab", split_axis=3, concat_axis=2, tiled=True),
    )
    summed = lax.psum(partial_image, "coil")
    portion = summed.shape[1] // lax.axis_size("coil")
    summed = lax.dynamic_slice_in_dim(summed, lax.axis_index("coil") * portion, portion, 1)
    return summed.astype(jnp.bfloat16)


def solution(mesh):
    in_specs = (
        P(None, None, "slab", None),
        P("coil", None, "slab", None),
        P(None, "coil", "slab", None, None),
        P(None, "slab", None),
    )
    out_specs = P(None, "coil", "slab", None)
    return jax.shard_map(shards, mesh=mesh, in_specs=in_specs, out_specs=out_specs, check_vma=False)
```

profile of v0, /device:TPU:1, one launch (start us, length us, event | category | flops | bytes accessed | tf_op | source)
XLA Modules:
  0.0 1599.3 jit_solution(7993726364527364379)
XLA Ops:
  0.0 0.0 slice-start
  0.0 2.0 fusion.257
  2.0 0.0 slice-start.1
  2.0 8.3 copy.50
  10.4 0.0 slice-start.2
  10.4 8.6 fusion.72
  19.0 0.0 slice-done
  19.0 0.0 slice-done.1
  19.0 0.0 slice-done.2
  19.0 9.1 fusion.56
  28.1 9.1 fusion.59
  37.2 44.6 %fusion.8 = f32[2,4,32,128,320]{3,4,2,1,0:T(8,128)} fusion(f32[2,320,32,128]{3,1,2,0:T(8,128)} %fusion.72, f32[4,320,32,128]{3,1,2,0:T(8,128)} %fusion.59, f32[2,320,32,128]{3,1,2,0:T(8,128)} %copy.50, f32[4,320,32,128]{3,1,2,0:T(8,128)} %fusion.56), kind=kOutput, calls=%fused_computation.12 | convolution fusion | flops 6753955840 | bytes 104857600 | tf_op jit(solution)/shard_map/ky,scyzl->sckzl/dot_general | solution.py:55
  81.8 43.1 %fusion.9 = bf16[2,4,320,32,128]{4,2,3,1,0:T(8,128)(2,1)} fusion(f32[2,4,32,128,320]{3,4,2,1,0:T(8,128)} %fusion.8, f32[2,320,32,128]{3,1,2,0:T(8,128)} %fusion.72, f32[4,320,32,128]{3,1,2,0:T(8,128)} %fusion.59, f32[2,320,32,128]{3,1,2,0:T(8,128)} %copy.50, f32[4,320,32,128]{3,1,2,0:T(8,128)} %fusion.56, s32[128]{0:T(128)S(1)} %iota_add_fusion, ...), kind=kOutput, calls=%fused_computation.13 | convolution fusion | flops 9468772352 | bytes 126034560 | tf_op jit(solution)/shard_map/ky,scyzl->sckzl/dot_general | solution.py:56
  124.9 21.4 %copy.55 = bf16[2,4,320,32,128]{4,3,1,0,2:T(8,128)(2,1)} copy(bf16[2,4,320,32,128]{4,2,3,1,0:T(8,128)(2,1)} %fusion.9) | data formatting | bytes 41943040 | tf_op jit(solution)/shard_map/convert_element_type | solution.py:57
  146.3 6.8 all-to-all-start
  153.2 0.0 copy-start
  153.2 13.7 copy.60
  166.9 1.0 fusion.263
  167.9 1.0 fusion.261
  168.9 0.0 copy-done
  169.0 437.4 %all-to-all-done = bf16[2,4,320,32,128]{4,3,1,0,2:T(8,128)(2,1)} async-done(((bf16[2,4,320,32,128]{4,3,1,0,2:T(8,128)(2,1)}), bf16[2,4,320,32,128]{4,3,1,0,2:T(8,128)(2,1)}, u32[]{:S(2)}, u32[]{:S(2)}) %all-to-all-start) | async-done | bytes 20971552 | tf_op jit(solution)/shard_map/all_to_all | solution.py:99
  606.3 19.2 %copy.57 = bf16[2,4,40,8,32,128]{5,4,3,2,1,0:T(8,128)(2,1)} copy(bf16[2,4,40,8,32,128]{5,4,1,0,2,3:T(8,128)(2,1)} %bitcast.16) | data formatting | bytes 41943040 | tf_op jit(solution)/shard_map/all_to_all | solution.py:99
  625.5 21.7 %fusion.98 = f32[2,4,40,128,256]{4,3,2,1,0:T(8,128)} fusion(bf16[2,4,40,256,128]{4,3,2,1,0:T(8,128)(2,1)} %bitcast.172), kind=kOutput, calls=%fused_computation.86 | convolution fusion | flops 5369757696 | bytes 62914560 | tf_op jit(solution)/shard_map/jq,sckql->sckjl/dot_general | solution.py:69
  647.3 24.3 %fusion.21 = f32[2,4,40,128,256]{4,3,2,1,0:T(8,128)} fusion(bf16[2,4,40,256,128]{4,3,2,1,0:T(8,128)(2,1)} %bitcast.173, s32[128]{0:T(128)S(1)} %iota_add_fusion, pred[128]{0:T(512)(128)(4,1)S(1)} %iota_compare_fusion.4, bf16[256,256,1,1,1]{1,0,4,3,2:T(8,128)(2,1)S(1)} %fusion.263), kind=kOutput, calls=%fused_computation.25 | convolution fusion | flops 8063680512 | bytes 63046272 | tf_op jit(solution)/shard_map/jq,sckql->sckjl/dot_general | solution.py:71
  671.6 38.0 %fusion.12 = bf16[2,4,40,128,128]{3,4,2,1,0:T(8,128)(2,1)} fusion(bf16[2,4,40,128,128]{3,4,2,1,0:T(8,128)(2,1)} %copy.60, pred[2,40,128]{2,1,0:T(8,128)(4,1)S(1)} %broadcast_compare_fusion, f32[2,4,40,128,256]{4,3,2,1,0:T(8,128)} %fusion.98, f32[2,4,40,128,256]{4,3,2,1,0:T(8,128)} %fusion.21, s32[2,40,128]{2,1,0:T(8,128)S(1)} %broadcast_maximum_fusion), kind=kOutput, calls=%fused_computation.17 | convolution fusion | flops 16142827520 | bytes 104908800 | tf_op jit(solution)/shard_map/skjq,sckql->sckjl/dot_general | solution.py:72
  709.6 13.7 convert_bitcast_fusion
  723.2 28.2 %fusion.17 = f32[2,4,40,128,256]{4,3,2,1,0:T(8,128)} fusion(bf16[2,4,40,256,128]{3,4,1,2,0:T(8,128)(2,1)} %convert_bitcast_fusion, s32[128]{0:T(128)S(1)} %iota_add_fusion, pred[128]{0:T(512)(128)(4,1)S(1)} %iota_compare_fusion.4, bf16[256,256,1,1,1]{1,0,4,3,2:T(8,128)(2,1)S(1)} %fusion.261), kind=kOutput, calls=%fused_computation.21 | convolution fusion | flops 8063680512 | bytes 63046272 | tf_op jit(solution)/shard_map/qz,sckql->sckzl/dot_general | solution.py:82
  751.5 29.8 %fusion.10 = bf16[2,4,40,256,128]{3,4,2,1,0:T(8,128)(2,1)} fusion(f32[2,4,40,128,256]{4,3,2,1,0:T(8,128)} %fusion.17, bf16[2,4,40,256,128]{3,4,1,2,0:T(8,128)(2,1)} %convert_bitcast_fusion), kind=kOutput, calls=%fused_computation.14 | convolution fusion | flops 5390729216 | bytes 83886080 | tf_op jit(solution)/shard_map/qz,sckql->sckzl/dot_general | solution.py:81
  781.3 30.6 %copy.65 = bf16[2,4,40,256,128]{4,2,1,0,3:T(8,128)(2,1)} copy(bf16[2,4,40,256,128]{3,4,2,1,0:T(8,128)(2,1)} %fusion.10) | data formatting | bytes 41943040 | tf_op jit(solution)/shard_map/convert_element_type | solution.py:83
  811.9 6.1 all-to-all-start.1
  818.1 2.0 fusion.259
  820.0 449.4 %all-to-all-done.1 = bf16[2,4,40,256,128]{4,2,1,0,3:T(8,128)(2,1)} async-done(((bf16[2,4,40,256,128]{4,2,1,0,3:T(8,128)(2,1)}), bf16[2,4,40,256,128]{4,2,1,0,3:T(8,128)(2,1)}, u32[]{:S(2)}, u32[]{:S(2)}) %all-to-all-start.1) | async-done | bytes 20971552 | tf_op jit(solution)/shard_map/all_to_all | solution.py:100
  1269.5 19.4 %copy.67 = bf16[2,4,8,40,32,128]{5,3,2,4,1,0:T(8,128)(2,1)} copy(bf16[2,4,8,40,32,128]{5,3,1,0,4,2:T(8,128)(2,1)} %bitcast.33) | data formatting | bytes 41943040 | tf_op jit(solution)/shard_map/all_to_all | solution.py:100
  1288.9 26.3 %fusion.90 = f32[2,4,32,128,320]{3,4,2,1,0:T(8,128)} fusion(bf16[2,4,320,32,128]{4,2,3,1,0:T(8,128)(2,1)} %bitcast.170), kind=kOutput, calls=%fused_computation.83 | convolution fusion | flops 6712012800 | bytes 62914560 | tf_op jit(solution)/shard_map/ky,sckzl->scyzl/dot_general | solution.py:86
  1315.2 27.4 %fusion.13 = f32[2,4,32,128,320]{3,4,2,1,0:T(8,128)} fusion(bf16[2,4,320,32,128]{4,2,3,1,0:T(8,128)(2,1)} %bitcast.171, s32[128]{0:T(128)S(1)} %iota_add_fusion, pred[128]{0:T(512)(128)(4,1)S(1)} %iota_compare_fusion.4, bf16[320,320,1,1,1]{0,1,4,3,2:T(8,128)(2,1)S(1)} %fusion.259), kind=kOutput, calls=%fused_computation.18 | convolution fusion | flops 9405857792 | bytes 63120000 | tf_op jit(solution)/shard_map/ky,sckzl->scyzl/dot_general | solution.py:88
  1342.6 69.9 %fusion.3 = f32[2,320,32,128]{3,1,2,0:T(8,128)} fusion(f32[4,320,32,128]{3,1,2,0:T(8,128)} %fusion.59, f32[4,320,32,128]{3,1,2,0:T(8,128)} %fusion.56, f32[2,4,32,128,320]{3,4,2,1,0:T(8,128)} %fusion.90, f32[2,4,32,128,320]{3,4,2,1,0:T(8,128)} %fusion.13, s32[128]{0:T(128)S(1)} %iota_add_fusion, pred[128]{0:T(512)(128)(4,1)S(1)} %iota_compare_fusion.4), kind=kOutput, calls=%fused_computation.4 | convolution fusion | flops 16166551552 | bytes 136315520 | tf_op jit(solution)/shard_map/...l,lm->...m/dot_general | solution.py:39
  1412.5 183.5 %all-reduce.1 = bf16[2,320,32,128]{3,1,2,0:T(8,128)(2,1)} all-reduce(f32[2,320,32,128]{3,1,2,0:T(8,128)} %fusion.3), channel_id=1, replica_groups=mesh['slab'=8,'coil'=4] {'coil'}, use_global_device_ids=true, to_apply=%region_1.2 | all-reduce | flops 2621440 | bytes 15728640 | tf_op jit(solution)/shard_map/psum | solution.py:102
  1596.1 1.4 dynamic-slice_convert_fusion
  1597.5 1.4 copy.70
  (7 shorter events, 0.0 us)
Async XLA Ops:
  0.0 19.0 %slice-start = ((s8[10485760]{0:T(1024)(128)(4,1)}), s8[4194304]{0:T(1024)(128)(4,1)S(1)}, s32[]{:S(2)}) async-start(s8[10485760]{0:T(1024)(128)(4,1)} %bitcast.174), calls=%async_computation.2 | async-start | bytes 8388608
  2.0 17.0 %slice-start.1 = ((s8[10485760]{0:T(1024)(128)(4,1)}), s8[4194304]{0:T(1024)(128)(4,1)S(1)}, s32[]{:S(2)}) async-start(s8[10485760]{0:T(1024)(128)(4,1)} %bitcast.174), calls=%async_computation.3 | async-start | bytes 8388608
  10.4 8.6 slice-start.2
  146.3 460.0 %all-to-all-start = ((bf16[2,4,320,32,128]{4,3,1,0,2:T(8,128)(2,1)}), bf16[2,4,320,32,128]{4,3,1,0,2:T(8,128)(2,1)}, u32[]{:S(2)}, u32[]{:S(2)}) async-start(bf16[2,4,320,32,128]{4,3,1,0,2:T(8,128)(2,1)} %copy.55), calls=%async_computation | async-start | bytes 41943040 | tf_op jit(solution)/shard_map/all_to_all | solution.py:99
  153.2 15.7 copy-start
  811.9 457.5 %all-to-all-start.1 = ((bf16[2,4,40,256,128]{4,2,1,0,3:T(8,128)(2,1)}), bf16[2,4,40,256,128]{4,2,1,0,3:T(8,128)(2,1)}, u32[]{:S(2)}, u32[]{:S(2)}) async-start(bf16[2,4,40,256,128]{4,2,1,0,3:T(8,128)(2,1)} %copy.65), calls=%async_computation.1 | async-start | bytes 41943040 | tf_op jit(solution)/shard_map/all_to_all | solution.py:100
where the time goes:
time: 1610 us; the launch traced here: 1600 us
  waiting for transfers between devices  887 us (55%)
  matrix products  394 us (24%)
  blocking collectives  184 us (11%)
  local copies, waits for them, and re-layouts  116 us (7%)
    all_to_all x1, waiting for transfers between devices, shards(): lax.all_to_all(payload, 'slab', split_axis=3, concat_axis=2, tiled=True)  449 us
    all_to_all x1, waiting for transfers between devices, shards(): lax.all_to_all(payload, 'slab', split_axis=2, concat_axis=3, tiled=True)  437 us
    psum x1, blocking collectives, shards(): summed = lax.psum(partial_image, 'coil')  184 us
    dot_general x1, matrix products, lane_map(): jnp.einsum('...l,lm->...m', values, table.astype(jnp.float32), precision=...  69.9 us
    dot_general x1, matrix products, transform(): jnp.einsum('ky,scyzl->sckzl', y_cos, coil_image, preferred_element_type=j...  44.6 us
    dot_general x1, matrix products, transform(): jnp.einsum('ky,scyzl->sckzl', y_sin, turned_image, preferred_element_type...  43.1 us
    dot_general x1, matrix products, transform(): jnp.einsum('skjq,sckql->sckjl', onehot.astype(jnp.float32), kspace, preci...  38 us
  transfers between devices with their start and end apart: 2, of which 2 were waited for; matrix products, arithmetic and copies ran while one was open for 1% of the time, Pallas kernels for 0%

commit v1 on v0

--- a/solution.py
+++ b/solution.py
@@ -99,7 +99,8 @@
         lambda payload: lax.all_to_all(payload, "slab", split_axis=2, concat_axis=3, tiled=True),
         lambda payload: lax.all_to_all(payload, "slab", split_axis=3, concat_axis=2, tiled=True),
     )
-    summed = lax.psum(partial_image, "coil")
+    parts = lax.all_gather(partial_image, "coil")
+    summed = jnp.sum(parts, axis=0)
     portion = summed.shape[1] // lax.axis_size("coil")
     summed = lax.dynamic_slice_in_dim(summed, lax.axis_index("coil") * portion, portion, 1)
     return summed.astype(jnp.bfloat16)

time: 1610 us -> 1720 us (1.068)
  waiting for transfers between devices: 887 us -> 1140 us
  blocking collectives: 184 us -> 0 us
  other arithmetic: 5.94 us -> 25.4 us
    all_gather x0 -> x1, waiting for transfers between devices: none -> 251 us  [shards(): parts = lax.all_gather(partial_image, 'coil')]
    psum x1 -> x0, blocking collectives: 184 us -> none  [shards(): summed = lax.psum(partial_image, 'coil')]
    reduce_sum x0 -> x1, other arithmetic: none -> 19.5 us  [shards(): summed = jnp.sum(parts, axis=0)]
  transfers between devices with their start and end apart: 2 -> 3, of which waited for: 2 -> 3; matrix products, arithmetic and copies ran while one was open for 1% -> 1% of each run, Pallas kernels for 0% -> 0%
where the time goes in v1:
time: 1720 us
  waiting for transfers between devices  1140 us (66%)
  matrix products  394 us (23%)
  local copies, waits for them, and re-layouts  131 us (8%)
  other arithmetic  25.4 us (1%)
    all_to_all x1, waiting for transfers between devices, shards(): lax.all_to_all(payload, 'slab', split_axis=3, concat_axis=2, tiled=True)  449 us
    all_to_all x1, waiting for transfers between devices, shards(): lax.all_to_all(payload, 'slab', split_axis=2, concat_axis=3, tiled=True)  437 us
    all_gather x1, waiting for transfers between devices, shards(): parts = lax.all_gather(partial_image, 'coil')  251 us
    dot_general x1, matrix products, lane_map(): jnp.einsum('...l,lm->...m', values, table.astype(jnp.float32), precision=...  69.9 us
    dot_general x1, matrix products, transform(): jnp.einsum('ky,scyzl->sckzl', y_cos, coil_image, preferred_element_type=j...  44.6 us
    dot_general x1, matrix products, transform(): jnp.einsum('ky,scyzl->sckzl', y_sin, turned_image, preferred_element_type...  43.1 us
    dot_general x1, matrix products, transform(): jnp.einsum('skjq,sckql->sckjl', onehot.astype(jnp.float32), kspace, preci...  38 us
  transfers between devices with their start and end apart: 3, of which 3 were waited for; matrix products, arithmetic and copies ran while one was open for 1% of the time, Pallas kernels for 0%

profile of v1, /device:TPU:1, one launch (start us, length us, event | category | flops | bytes accessed | tf_op | source)
XLA Modules:
  0.0 1715.8 jit_solution(12390046690667672285)
XLA Ops:
  6.5 0.0 slice-start
  6.6 2.0 fusion.257
  8.5 0.0 slice-start.1
  8.5 8.3 copy.50
  16.9 0.0 slice-start.2
  16.9 8.6 fusion.72
  25.5 0.0 slice-done
  25.5 0.0 slice-done.1
  25.5 0.0 slice-done.2
  25.5 9.1 fusion.56
  34.6 9.1 fusion.59
  43.7 44.6 %fusion.8 = f32[2,4,32,128,320]{3,4,2,1,0:T(8,128)} fusion(f32[2,320,32,128]{3,1,2,0:T(8,128)} %fusion.72, f32[4,320,32,128]{3,1,2,0:T(8,128)} %fusion.59, f32[2,320,32,128]{3,1,2,0:T(8,128)} %copy.50, f32[4,320,32,128]{3,1,2,0:T(8,128)} %fusion.56), kind=kOutput, calls=%fused_computation.12 | convolution fusion | flops 6753955840 | bytes 104857600 | tf_op jit(solution)/shard_map/ky,scyzl->sckzl/dot_general | solution.py:55
  88.3 43.1 %fusion.9 = bf16[2,4,320,32,128]{4,2,3,1,0:T(8,128)(2,1)} fusion(f32[2,4,32,128,320]{3,4,2,1,0:T(8,128)} %fusion.8, f32[2,320,32,128]{3,1,2,0:T(8,128)} %fusion.72, f32[4,320,32,128]{3,1,2,0:T(8,128)} %fusion.59, f32[2,320,32,128]{3,1,2,0:T(8,128)} %copy.50, f32[4,320,32,128]{3,1,2,0:T(8,128)} %fusion.56, s32[128]{0:T(128)S(1)} %iota_add_fusion, ...), kind=kOutput, calls=%fused_computation.13 | convolution fusion | flops 9468772352 | bytes 126034560 | tf_op jit(solution)/shard_map/ky,scyzl->sckzl/dot_general | solution.py:56
  131.5 21.4 %copy.55 = bf16[2,4,320,32,128]{4,3,1,0,2:T(8,128)(2,1)} copy(bf16[2,4,320,32,128]{4,2,3,1,0:T(8,128)(2,1)} %fusion.9) | data formatting | bytes 41943040 | tf_op jit(solution)/shard_map/convert_element_type | solution.py:57
  152.9 6.8 all-to-all-start
  159.7 0.0 copy-start
  159.7 13.8 copy.60
  173.6 1.0 fusion.263
  174.6 1.0 fusion.261
  175.5 0.0 copy-done
  175.6 437.3 %all-to-all-done = bf16[2,4,320,32,128]{4,3,1,0,2:T(8,128)(2,1)} async-done(((bf16[2,4,320,32,128]{4,3,1,0,2:T(8,128)(2,1)}), bf16[2,4,320,32,128]{4,3,1,0,2:T(8,128)(2,1)}, u32[]{:S(2)}, u32[]{:S(2)}) %all-to-all-start) | async-done | bytes 20971552 | tf_op jit(solution)/shard_map/all_to_all | solution.py:99
  612.9 19.2 %copy.57 = bf16[2,4,40,8,32,128]{5,4,3,2,1,0:T(8,128)(2,1)} copy(bf16[2,4,40,8,32,128]{5,4,1,0,2,3:T(8,128)(2,1)} %bitcast.16) | data formatting | bytes 41943040 | tf_op jit(solution)/shard_map/all_to_all | solution.py:99
  632.2 21.7 %fusion.98 = f32[2,4,40,128,256]{4,3,2,1,0:T(8,128)} fusion(bf16[2,4,40,256,128]{4,3,2,1,0:T(8,128)(2,1)} %bitcast.173), kind=kOutput, calls=%fused_computation.86 | convolution fusion | flops 5369757696 | bytes 62914560 | tf_op jit(solution)/shard_map/jq,sckql->sckjl/dot_general | solution.py:69
  653.9 24.3 %fusion.21 = f32[2,4,40,128,256]{4,3,2,1,0:T(8,128)} fusion(bf16[2,4,40,256,128]{4,3,2,1,0:T(8,128)(2,1)} %bitcast.174, s32[128]{0:T(128)S(1)} %iota_add_fusion, pred[128]{0:T(512)(128)(4,1)S(1)} %iota_compare_fusion.4, bf16[256,256,1,1,1]{1,0,4,3,2:T(8,128)(2,1)S(1)} %fusion.263), kind=kOutput, calls=%fused_computation.25 | convolution fusion | flops 8063680512 | bytes 63046272 | tf_op jit(solution)/shard_map/jq,sckql->sckjl/dot_general | solution.py:71
  678.2 38.0 %fusion.12 = bf16[2,4,40,128,128]{3,4,2,1,0:T(8,128)(2,1)} fusion(bf16[2,4,40,128,128]{3,4,2,1,0:T(8,128)(2,1)} %copy.60, pred[2,40,128]{2,1,0:T(8,128)(4,1)S(1)} %broadcast_compare_fusion, f32[2,4,40,128,256]{4,3,2,1,0:T(8,128)} %fusion.98, f32[2,4,40,128,256]{4,3,2,1,0:T(8,128)} %fusion.21, s32[2,40,128]{2,1,0:T(8,128)S(1)} %broadcast_maximum_fusion), kind=kOutput, calls=%fused_computation.17 | convolution fusion | flops 16142827520 | bytes 104908800 | tf_op jit(solution)/shard_map/skjq,sckql->sckjl/dot_general | solution.py:72
  716.2 13.6 convert_bitcast_fusion
  729.9 28.2 %fusion.17 = f32[2,4,40,128,256]{4,3,2,1,0:T(8,128)} fusion(bf16[2,4,40,256,128]{3,4,1,2,0:T(8,128)(2,1)} %convert_bitcast_fusion, s32[128]{0:T(128)S(1)} %iota_add_fusion, pred[128]{0:T(512)(128)(4,1)S(1)} %iota_compare_fusion.4, bf16[256,256,1,1,1]{1,0,4,3,2:T(8,128)(2,1)S(1)} %fusion.261), kind=kOutput, calls=%fused_computation.21 | convolution fusion | flops 8063680512 | bytes 63046272 | tf_op jit(solution)/shard_map/qz,sckql->sckzl/dot_general | solution.py:82
  758.1 29.8 %fusion.10 = bf16[2,4,40,256,128]{3,4,2,1,0:T(8,128)(2,1)} fusion(f32[2,4,40,128,256]{4,3,2,1,0:T(8,128)} %fusion.17, bf16[2,4,40,256,128]{3,4,1,2,0:T(8,128)(2,1)} %convert_bitcast_fusion), kind=kOutput, calls=%fused_computation.14 | convolution fusion | flops 5390729216 | bytes 83886080 | tf_op jit(solution)/shard_map/qz,sckql->sckzl/dot_general | solution.py:81
  787.9 32.6 %copy.65 = bf16[2,4,40,256,128]{4,2,1,0,3:T(8,128)(2,1)} copy(bf16[2,4,40,256,128]{3,4,2,1,0:T(8,128)(2,1)} %fusion.10) | data formatting | bytes 41943040 | tf_op jit(solution)/shard_map/convert_element_type | solution.py:83
  820.5 6.1 all-to-all-start.1
  826.6 0.0 all-gather.3.cloned.1.call-start
  826.7 2.0 fusion.259
  828.6 449.4 %all-to-all-done.1 = bf16[2,4,40,256,128]{4,2,1,0,3:T(8,128)(2,1)} async-done(((bf16[2,4,40,256,128]{4,2,1,0,3:T(8,128)(2,1)}), bf16[2,4,40,256,128]{4,2,1,0,3:T(8,128)(2,1)}, u32[]{:S(2)}, u32[]{:S(2)}) %all-to-all-start.1) | async-done | bytes 20971552 | tf_op jit(solution)/shard_map/all_to_all | solution.py:100
  1278.1 19.4 %copy.67 = bf16[2,4,8,40,32,128]{5,3,2,4,1,0:T(8,128)(2,1)} copy(bf16[2,4,8,40,32,128]{5,3,1,0,4,2:T(8,128)(2,1)} %bitcast.33) | data formatting | bytes 41943040 | tf_op jit(solution)/shard_map/all_to_all | solution.py:100
  1297.5 26.6 %fusion.90 = f32[2,4,32,128,320]{3,4,2,1,0:T(8,128)} fusion(bf16[2,4,320,32,128]{4,2,3,1,0:T(8,128)(2,1)} %bitcast.171), kind=kOutput, calls=%fused_computation.83 | convolution fusion | flops 6712012800 | bytes 62914560 | tf_op jit(solution)/shard_map/ky,sckzl->scyzl/dot_general | solution.py:86
  1324.1 27.4 %fusion.13 = f32[2,4,32,128,320]{3,4,2,1,0:T(8,128)} fusion(bf16[2,4,320,32,128]{4,2,3,1,0:T(8,128)(2,1)} %bitcast.172, s32[128]{0:T(128)S(1)} %iota_add_fusion, pred[128]{0:T(512)(128)(4,1)S(1)} %iota_compare_fusion.4, bf16[320,320,1,1,1]{0,1,4,3,2:T(8,128)(2,1)S(1)} %fusion.259), kind=kOutput, calls=%fused_computation.18 | convolution fusion | flops 9405857792 | bytes 63120000 | tf_op jit(solution)/shard_map/ky,sckzl->scyzl/dot_general | solution.py:88
  1351.5 69.9 %fusion.3 = f32[2,320,32,128]{3,1,2,0:T(8,128)} fusion(f32[4,320,32,128]{3,1,2,0:T(8,128)} %fusion.59, f32[4,320,32,128]{3,1,2,0:T(8,128)} %fusion.56, f32[2,4,32,128,320]{3,4,2,1,0:T(8,128)} %fusion.90, f32[2,4,32,128,320]{3,4,2,1,0:T(8,128)} %fusion.13, s32[128]{0:T(128)S(1)} %iota_add_fusion, pred[128]{0:T(512)(128)(4,1)S(1)} %iota_compare_fusion.4), kind=kOutput, calls=%fused_computation.4 | convolution fusion | flops 16166551552 | bytes 136315520 | tf_op jit(solution)/shard_map/...l,lm->...m/dot_general | solution.py:39
  1421.4 14.0 copy.70
  1435.4 0.0 all-gather.3.cloned.1.call-update
  1435.4 251.0 %all-gather.3.cloned.1.call-done = f32[8,320,32,128]{3,2,1,0:T(8,128)} async-done(((f32[2,320,32,128]{3,2,1,0:T(8,128)}), f32[8,320,32,128]{3,2,1,0:T(8,128)}) %all-gather.3.cloned.1.call-update) | async-done | bytes 41943056 | tf_op jit(solution)/shard_map/all_gather | solution.py:102
  1686.4 19.5 %reduce_sum.19 = bf16[2,320,32,128]{3,2,1,0:T(8,128)(2,1)} reduce(f32[4,2,320,32,128]{4,3,2,1,0:T(8,128)} %bitcast.177, f32[]{:T(128)} %constant.63.clone.1), dimensions={0}, to_apply=%region_1.2 | reduce | flops 7864320 | bytes 47185924 | tf_op jit(solution)/shard_map/reduce_sum | solution.py:103
  1705.9 2.6 dynamic-slice_convert_fusion
  (7 shorter events, 0.0 us)
Async XLA Ops:
  6.5 19.0 %slice-start = ((s8[10485760]{0:T(1024)(128)(4,1)}), s8[4194304]{0:T(1024)(128)(4,1)S(1)}, s32[]{:S(2)}) async-start(s8[10485760]{0:T(1024)(128)(4,1)} %bitcast.175), calls=%async_computation.3 | async-start | bytes 8388608
  8.5 17.0 slice-start.1
  16.9 8.6 slice-start.2
  152.9 460.0 %all-to-all-start = ((bf16[2,4,320,32,128]{4,3,1,0,2:T(8,128)(2,1)}), bf16[2,4,320,32,128]{4,3,1,0,2:T(8,128)(2,1)}, u32[]{:S(2)}, u32[]{:S(2)}) async-start(bf16[2,4,320,32,128]{4,3,1,0,2:T(8,128)(2,1)} %copy.55), calls=%async_computation | async-start | bytes 41943040 | tf_op jit(solution)/shard_map/all_to_all | solution.py:99
  159.7 15.8 copy-start
  820.5 457.5 %all-to-all-start.1 = ((bf16[2,4,40,256,128]{4,2,1,0,3:T(8,128)(2,1)}), bf16[2,4,40,256,128]{4,2,1,0,3:T(8,128)(2,1)}, u32[]{:S(2)}, u32[]{:S(2)}) async-start(bf16[2,4,40,256,128]{4,2,1,0,3:T(8,128)(2,1)} %copy.65), calls=%async_computation.1 | async-start | bytes 41943040 | tf_op jit(solution)/shard_map/all_to_all | solution.py:100
  826.6 859.8 %all-gather.3.cloned.1.call-start = ((), (), s32[]{:S(2)}) async-start(), calls=%async_computation.2 | async-start | bytes 52428800 | tf_op jit(solution)/shard_map/all_gather | solution.py:102
Sparse Core Ops, SparseCore 0:
  1435.5 250.8 all-gather.2
